TPU v7x, 512 devices: a whole 4x4x16 slice. The times are simulated.
512 devices in a mesh: patch: 128 (over z, y, core), mp: 4 (over x).
Axes of the slice: x: 4, y: 4, z: 16, core: 2. Of those that a mesh axis runs over, the one named last changes fastest.
Arguments:
- features: bfloat16 [65536, 1024], P('patch'), may hold values from -16 to 16
- gain_attn: float32 [1024], replicated, may hold values from 0.1 to 1.9
- w_qkv: bfloat16 [3, 1024, 1024], P(None, None, 'mp'), as said below
- w_out: bfloat16 [1024, 1024], P('mp'), may hold values from -0.1875 to 0.1875
- gain_mlp: float32 [1024], replicated, may hold values from 0.1 to 1.9
- w_up: bfloat16 [1024, 2048], P(None, 'mp'), may hold values from -0.1875 to 0.1875
- w_down: bfloat16 [2048, 1024], P('mp'), may hold values from -0.125 to 0.125
- neighbours: int32 [512, 8], replicated, may hold values from 0 to 511, as said below
Outputs:
- layer_out: bfloat16 [65536, 1024], P('patch', 'mp')
Inputs may be any that keep to these rules, and one draw needn't show every extreme that they name: `neighbours`: row p lists 8 different patches; the first is p itself. Patch q belongs to device q // 4 of the patch axis, and every listed patch belongs to a device whose index differs from that of p's device by at most 2 around the patch axis (the lining closes into a cycle). `w_qkv`: projection weights of mean zero.
All inputs are finite; a program needn't handle non-finite values.
Results may differ from a plain program's by a relative error of at most 0.012.
Values may be sent and summed in bfloat16 or wider, within the bound.
No kernel may reach another device: no remote copies, remote signals or barrier semaphores. Data moves between devices by JAX's collectives and lax.ppermute only.
A program may use at most 64 MiB of HBM per device.

v0:
```python
import jax
import jax.numpy as jnp
from jax import lax
from jax.sharding import PartitionSpec as P

D = 1024
HD = 64
PN = 128
K_NB = 8
REACH = 2


def from_behind(array, axis, by):
    length = lax.axis_size(axis)
    return lax.ppermute(array, axis, [(i, (i + by) % length) for i in range(length)])


def normalize(rows, gain):
    rows32 = rows.astype(jnp.float32)
    mean_sq = jnp.mean(rows32 * rows32, axis=-1, keepdims=True)
    return (rows32 * lax.rsqrt(mean_sq + 1e-05) * gain).astype(jnp.bfloat16)


def per_device(features, gain_attn, w_qkv, w_out, gain_mlp, w_up, w_down, neighbours):
    row_count = features.shape[0]
    patches_here = row_count // PN
    heads_here = w_qkv.shape[2] // HD
    normed = normalize(features, gain_attn)
    queries = jnp.dot(normed, w_qkv[0], preferred_element_type=jnp.float32).astype(jnp.bfloat16)
    own_keys = (
        jnp.dot(normed, w_qkv[1], preferred_element_type=jnp.float32)
        .astype(jnp.bfloat16)
        .reshape(patches_here, PN, -1)
    )
    own_vals = (
        jnp.dot(normed, w_qkv[2], preferred_element_type=jnp.float32)
        .astype(jnp.bfloat16)
        .reshape(patches_here, PN, -1)
    )
    window = {0: (own_keys, own_vals)}
    for offset in range(-REACH, REACH + 1):
        if offset != 0:
            window[offset] = from_behind((own_keys, own_vals), "patch", -offset)
    keys_win = jnp.concatenate([window[offset][0] for offset in range(-REACH, REACH + 1)], axis=0)
    vals_win = jnp.concatenate([window[offset][1] for offset in range(-REACH, REACH + 1)], axis=0)
    device = lax.axis_index("patch")
    n_dev = lax.axis_size("patch")
    listed = lax.dynamic_slice_in_dim(neighbours, device * patches_here, patches_here, 0)
    owner_dev = listed // patches_here
    offset_dev = jnp.mod(owner_dev - device + n_dev // 2, n_dev) - n_dev // 2
    slot_index = (offset_dev + REACH) * patches_here + jnp.mod(listed, patches_here)
    keys_nb = keys_win[slot_index].reshape(patches_here, K_NB * PN, heads_here, HD)
    vals_nb = vals_win[slot_index].reshape(patches_here, K_NB * PN, heads_here, HD)
    query_blk = queries.reshape(patches_here, PN, heads_here, HD)
    scores = jnp.einsum(
        "pqhd,pkhd->phqk", query_blk, keys_nb, preferred_element_type=jnp.float32
    ) * (1.0 / HD**0.5)
    probs = jax.nn.softmax(scores, axis=-1).astype(jnp.bfloat16)
    mixed_rows = jnp.einsum("phqk,pkhd->pqhd", probs, vals_nb, preferred_element_type=jnp.float32)
    attended = mixed_rows.astype(jnp.bfloat16).reshape(row_count, heads_here * HD)
    partial_value = jnp.dot(attended, w_out, preferred_element_type=jnp.float32)
    col_share = lax.psum_scatter(
        partial_value.astype(jnp.bfloat16), "mp", scatter_dimension=1, tiled=True
    ).astype(jnp.float32)
    col_width = col_share.shape[1]
    col_begin = lax.axis_index("mp") * col_width
    residual_cols = (
        lax.dynamic_slice_in_dim(features, col_begin, col_width, 1).astype(jnp.float32) + col_share
    )
    gain_cols = lax.dynamic_slice_in_dim(gain_mlp, col_begin, col_width, 0)
    square_sum = lax.psum(jnp.sum(residual_cols * residual_cols, axis=1), "mp")
    inverse_rms = lax.rsqrt(square_sum / D + 1e-05)
    normed_cols = (residual_cols * inverse_rms[:, None] * gain_cols).astype(jnp.bfloat16)
    normed2 = lax.all_gather(normed_cols, "mp", axis=1, tiled=True)
    hidden = jax.nn.gelu(
        jnp.dot(normed2, w_up, preferred_element_type=jnp.float32), approximate=True
    ).astype(jnp.bfloat16)
    down_term = jnp.dot(hidden, w_down, preferred_element_type=jnp.float32)
    down_cols = lax.psum_scatter(
        down_term.astype(jnp.bfloat16), "mp", scatter_dimension=1, tiled=True
    ).astype(jnp.float32)
    return (residual_cols + down_cols).astype(jnp.bfloat16)


def solution(mesh):
    return jax.shard_map(
        per_device,
        mesh=mesh,
        in_specs=(
            P("patch", None),
            P(),
            P(None, None, "mp"),
            P("mp", None),
            P(),
            P(None, "mp"),
            P("mp", None),
            P(),
        ),
        out_specs=P("patch", "mp"),
        check_vma=False,
    )
```

profile of v0, /device:TPU:8, one launch (start us, length us, event | category | flops | bytes accessed | tf_op | source)
XLA Modules:
  0.0 209.8 jit_solution(8594160232992480794)
XLA Ops:
  6.5 0.0 copy-start.6
  6.6 1.7 fusion.9
  8.2 1.9 convolution_convert_fusion.2
  10.1 3.5 %collective-permute-start.4 = (bf16[4,128,256]{2,1,0:T(8,128)(2,1)S(1)}, bf16[4,128,256]{2,1,0:T(8,128)(2,1)}, u32[]{:S(2)}, u32[]{:S(2)}) collective-permute-start(bf16[4,128,256]{2,1,0:T(8,128)(2,1)S(1)} %bitcast.30), channel_id=1, source_target_pairs={{0,8},{4,12},{8,16},{12,20},{16,24},{20,28},{24,32},{28,36},{32,40... | collective-permute-start | bytes 786440 | tf_op jit(solution)/shard_map/ppermute | solution.py:15
  13.6 1.9 collective-permute-start.5
  15.5 3.6 %collective-permute-start.6 = (bf16[4,128,256]{2,1,0:T(8,128)(2,1)S(1)}, bf16[4,128,256]{2,1,0:T(8,128)(2,1)S(1)}, u32[]{:S(2)}, u32[]{:S(2)}) collective-permute-start(bf16[4,128,256]{2,1,0:T(8,128)(2,1)S(1)} %bitcast.32), channel_id=1, source_target_pairs={{0,508},{4,0},{8,4},{12,8},{16,12},{20,16},{24,20},{28,24},{32,28}... | collective-permute-start | bytes 786440 | tf_op jit(solution)/shard_map/ppermute | solution.py:15
  19.2 10.4 %collective-permute-start.7 = (bf16[4,128,256]{2,1,0:T(8,128)(2,1)S(1)}, bf16[4,128,256]{2,1,0:T(8,128)(2,1)S(1)}, u32[]{:S(2)}, u32[]{:S(2)}) collective-permute-start(bf16[4,128,256]{2,1,0:T(8,128)(2,1)S(1)} %bitcast.33), channel_id=1, source_target_pairs={{0,504},{4,508},{8,0},{12,4},{16,8},{20,12},{24,16},{28,20},{32,24... | collective-permute-start | bytes 786440 | tf_op jit(solution)/shard_map/ppermute | solution.py:15
  29.6 0.0 copy-done.2
  29.6 0.0 copy-done.8
  29.6 0.0 copy-done.6
  29.7 0.5 convolution_convert_fusion.4
  30.1 1.9 collective-permute-start
  32.1 0.5 convolution_convert_fusion.3
  32.6 0.8 compare_select_fusion
  33.4 0.1 copy.17
  33.5 0.1 reshape.39
  33.5 1.0 reshape.60
  34.6 0.0 collective-permute-done.4
  34.6 1.9 collective-permute-start.1
  36.5 1.7 constant_dynamic-update-slice_fusion.9
  38.2 0.0 collective-permute-done.5
  38.2 3.6 %collective-permute-start.2 = (bf16[4,128,256]{2,1,0:T(8,128)(2,1)S(1)}, bf16[4,128,256]{2,1,0:T(8,128)(2,1)}, u32[]{:S(2)}, u32[]{:S(2)}) collective-permute-start(bf16[4,128,256]{2,1,0:T(8,128)(2,1)S(1)} %bitcast.27), channel_id=1, source_target_pairs={{0,508},{4,0},{8,4},{12,8},{16,12},{20,16},{24,20},{28,24},{32,28}... | collective-permute-start | bytes 786440 | tf_op jit(solution)/shard_map/ppermute | solution.py:15
  41.8 1.7 constant_dynamic-update-slice_fusion.8
  43.5 0.7 constant_dynamic-update-slice_fusion.7
  44.2 0.0 collective-permute-done.6
  44.2 7.5 %collective-permute-start.3 = (bf16[4,128,256]{2,1,0:T(8,128)(2,1)S(1)}, bf16[4,128,256]{2,1,0:T(8,128)(2,1)}, u32[]{:S(2)}, u32[]{:S(2)}) collective-permute-start(bf16[4,128,256]{2,1,0:T(8,128)(2,1)S(1)} %bitcast.28), channel_id=1, source_target_pairs={{0,504},{4,508},{8,0},{12,4},{16,8},{20,12},{24,16},{28,20},{32,24... | collective-permute-start | bytes 786440 | tf_op jit(solution)/shard_map/ppermute | solution.py:15
  51.7 0.7 constant_dynamic-update-slice_fusion.6
  52.4 0.0 collective-permute-done.7
  52.5 0.7 constant_dynamic-update-slice_fusion.5
  53.2 2.0 gather_fusion.1
  55.2 3.2 %reshape.61 = bf16[4,1024,4,64]{3,2,1,0:T(4,128)(2,1)} reshape(bf16[32,128,256]{2,1,0:T(8,128)(2,1)S(1)} %gather_fusion.1) | data formatting | bytes 4194304 | tf_op jit(solution)/shard_map/reshape | solution.py:52
  58.4 3.6 %fusion.4 = f32[4,4,128,1024]{3,2,1,0:T(8,128)S(1)} fusion(bf16[4,1024,4,64]{3,2,1,0:T(4,128)(2,1)} %reshape.61, bf16[4,128,4,64]{3,2,1,0:T(4,128)(2,1)} %reshape.60), kind=kOutput, calls=%fused_computation.7 | convolution fusion | flops 268435456 | bytes 10747904 | tf_op jit(solution)/shard_map/pqhd,pkhd->phqk/dot_general | solution.py:55
  62.1 2.2 %fusion.62 = f32[4,4,128]{2,1,0:T(4,128)S(1)} fusion(f32[4,4,128,1024]{3,2,1,0:T(8,128)S(1)} %fusion.4), kind=kOutput, calls=%fused_computation.87 | output fusion | flops 8389631 | bytes 8396800 | tf_op jit(solution)/shard_map/sub | solution.py:58
  64.2 1.0 copy-done.1
  65.3 0.0 collective-permute-done
  65.3 1.7 constant_dynamic-update-slice_fusion.4
  67.0 0.0 collective-permute-done.1
  67.0 1.7 constant_dynamic-update-slice_fusion.3
  68.6 0.7 constant_dynamic-update-slice_fusion.2
  69.4 0.0 collective-permute-done.2
  69.4 1.7 constant_dynamic-update-slice_fusion.1
  71.1 0.0 collective-permute-done.3
  71.1 1.7 constant_dynamic-update-slice_fusion
  72.7 2.0 gather_fusion
  74.7 3.3 %reshape.59 = bf16[4,1024,4,64]{3,2,1,0:T(4,128)(2,1)} reshape(bf16[32,128,256]{2,1,0:T(8,128)(2,1)S(1)} %gather_fusion) | data formatting | bytes 4194304 | tf_op jit(solution)/shard_map/reshape | solution.py:53
  78.0 12.1 %fusion.15 = bf16[4,128,4,64]{1,3,2,0:T(8,128)(2,1)S(1)} fusion(f32[4,4,128]{2,1,0:T(4,128)S(1)} %fusion.62, bf16[4,1024,4,64]{3,2,1,0:T(4,128)(2,1)} %reshape.59, f32[4,4,128,1024]{3,2,1,0:T(8,128)} %copy-done.1), kind=kOutput, calls=%fused_computation.24 | convolution fusion | flops 279055360 | bytes 10756096 | tf_op jit(solution)/shard_map/phqk,pkhd->pqhd/dot_general | solution.py:59
  90.1 0.0 copy-start.3
  90.2 0.2 copy.24
  90.4 1.4 convolution_convert_fusion
  91.8 0.0 reduce-scatter.3.cloned.1.call-update
  91.8 0.0 all-gather.2.cloned.1.call-start
  91.9 0.8 dynamic_slice.11
  92.7 28.3 %reduce-scatter.3.cloned.1.call-done = bf16[512,256]{1,0:T(8,128)(2,1)} async-done(((bf16[512,1024]{1,0:T(8,128)(2,1)}), bf16[512,256]{1,0:T(8,128)(2,1)}) %reduce-scatter.3.cloned.1.call-update) | async-done | bytes 262160 | tf_op jit(solution)/shard_map/reduce_scatter | solution.py:62
  121.1 1.1 multiply_reduce_fusion.1
  122.2 8.4 %psum.7 = f32[512]{0:T(512)S(1)} all-reduce(f32[512]{0:T(512)S(1)} %multiply_reduce_fusion.1), channel_id=1, replica_groups=mesh['patch'=128,'mp'=4] {'mp'}, use_global_device_ids=true, to_apply=%region_5.6 | all-reduce | flops 512 | bytes 4096 | tf_op jit(solution)/shard_map/psum | solution.py:71
  130.6 1.8 multiply_convert_fusion
  132.3 0.0 all-gather.2.cloned.1.call-update
  132.4 0.0 copy-start.4
  132.4 0.0 reduce-scatter.5.cloned.1.call-start
  132.4 32.9 %all-gather.2.cloned.1.call-done = bf16[512,1024]{1,0:T(8,128)(2,1)} async-done(((bf16[512,256]{1,0:T(8,128)(2,1)}), bf16[512,1024]{1,0:T(8,128)(2,1)}) %all-gather.2.cloned.1.call-update) | async-done | bytes 1048592 | tf_op jit(solution)/shard_map/all_gather | solution.py:74
  165.3 3.6 %convolution_convert_fusion.1 = bf16[512,1024]{1,0:T(8,128)(2,1)} fusion(bf16[512,1024]{1,0:T(8,128)(2,1)S(1)} %copy-done, bf16[512,1024]{1,0:T(8,128)(2,1)} %all-gather.2.cloned.1.call-done, bf16[1024,512]{1,0:T(8,128)(2,1)S(1)} %copy-done.7), kind=kOutput, calls=%fused_computation.19 | convolution fusion | flops 1076625408 | bytes 4194304 | tf_op jit(solution)/shard_map/dot_general | solution.py:78
  168.9 0.0 reduce-scatter.5.cloned.1.call-update
  168.9 32.6 %reduce-scatter.5.cloned.1.call-done = bf16[512,256]{1,0:T(8,128)(2,1)} async-done(((bf16[512,1024]{1,0:T(8,128)(2,1)}), bf16[512,256]{1,0:T(8,128)(2,1)}) %reduce-scatter.5.cloned.1.call-update) | async-done | bytes 262160 | tf_op jit(solution)/shard_map/reduce_scatter | solution.py:79
  201.5 1.8 add_convert_fusion
  (15 shorter events, 0.0 us)
Async XLA Ops:
  6.5 158.8 %copy-start = (bf16[512,1024]{1,0:T(8,128)(2,1)S(1)}, bf16[512,1024]{1,0:T(8,128)(2,1)}, u32[]{:S(2)}) copy-start(bf16[512,1024]{1,0:T(8,128)(2,1)} %param.14) | copy-start | bytes 3145732
  6.5 23.1 %copy-start.2 = (bf16[512,1024]{1,0:T(8,128)(2,1)S(1)}, bf16[512,1024]{1,0:T(8,128)(2,1)}, u32[]{:S(2)}) copy-start(bf16[512,1024]{1,0:T(8,128)(2,1)} %param.8) | copy-start | bytes 3145732
  6.5 23.1 %copy-start.8 = (f32[1024]{0:T(1024)S(1)}, f32[1024]{0:T(1024)}, u32[]{:S(2)}) copy-start(f32[1024]{0:T(1024)} %param.9) | copy-start | bytes 12292
  6.5 114.5 %reduce-scatter.3.cloned.1.call-start = ((), (), s32[]{:S(2)}) async-start(), calls=%async_computation.2 | async-start | bytes 1310720 | tf_op jit(solution)/shard_map/reduce_scatter | solution.py:62
  6.5 23.1 %copy-start.6 = (bf16[3,1024,256]{2,1,0:T(8,128)(2,1)S(1)}, bf16[3,1024,256]{2,1,0:T(8,128)(2,1)}, u32[]{:S(2)}) copy-start(bf16[3,1024,256]{2,1,0:T(8,128)(2,1)} %param.10) | copy-start | bytes 4718596
  10.1 24.5 %collective-permute-start.4 = (bf16[4,128,256]{2,1,0:T(8,128)(2,1)S(1)}, bf16[4,128,256]{2,1,0:T(8,128)(2,1)}, u32[]{:S(2)}, u32[]{:S(2)}) collective-permute-start(bf16[4,128,256]{2,1,0:T(8,128)(2,1)S(1)} %bitcast.30), channel_id=1, source_target_pairs={{0,8},{4,12},{8,16},{12,20},{16,24},{20,28},{24,32},{28,36},{32,40... | collective-permute-start | bytes 786440 | tf_op jit(solution)/shard_map/ppermute | solution.py:15
  13.6 24.6 %collective-permute-start.5 = (bf16[4,128,256]{2,1,0:T(8,128)(2,1)S(1)}, bf16[4,128,256]{2,1,0:T(8,128)(2,1)}, u32[]{:S(2)}, u32[]{:S(2)}) collective-permute-start(bf16[4,128,256]{2,1,0:T(8,128)(2,1)S(1)} %bitcast.31), channel_id=1, source_target_pairs={{0,4},{4,8},{8,12},{12,16},{16,20},{20,24},{24,28},{28,32},{32,36}... | collective-permute-start | bytes 786440 | tf_op jit(solution)/shard_map/ppermute | solution.py:15
  15.5 28.7 %collective-permute-start.6 = (bf16[4,128,256]{2,1,0:T(8,128)(2,1)S(1)}, bf16[4,128,256]{2,1,0:T(8,128)(2,1)S(1)}, u32[]{:S(2)}, u32[]{:S(2)}) collective-permute-start(bf16[4,128,256]{2,1,0:T(8,128)(2,1)S(1)} %bitcast.32), channel_id=1, source_target_pairs={{0,508},{4,0},{8,4},{12,8},{16,12},{20,16},{24,20},{28,24},{32,28}... | collective-permute-start | bytes 786440 | tf_op jit(solution)/shard_map/ppermute | solution.py:15
  19.2 33.3 %collective-permute-start.7 = (bf16[4,128,256]{2,1,0:T(8,128)(2,1)S(1)}, bf16[4,128,256]{2,1,0:T(8,128)(2,1)S(1)}, u32[]{:S(2)}, u32[]{:S(2)}) collective-permute-start(bf16[4,128,256]{2,1,0:T(8,128)(2,1)S(1)} %bitcast.33), channel_id=1, source_target_pairs={{0,504},{4,508},{8,0},{12,4},{16,8},{20,12},{24,16},{28,20},{32,24... | collective-permute-start | bytes 786440 | tf_op jit(solution)/shard_map/ppermute | solution.py:15
  30.1 35.1 %collective-permute-start = (bf16[4,128,256]{2,1,0:T(8,128)(2,1)S(1)}, bf16[4,128,256]{2,1,0:T(8,128)(2,1)}, u32[]{:S(2)}, u32[]{:S(2)}) collective-permute-start(bf16[4,128,256]{2,1,0:T(8,128)(2,1)S(1)} %bitcast.25), channel_id=1, source_target_pairs={{0,8},{4,12},{8,16},{12,20},{16,24},{20,28},{24,32},{28,36},{32,40... | collective-permute-start | bytes 786440 | tf_op jit(solution)/shard_map/ppermute | solution.py:15
  34.6 32.4 %collective-permute-start.1 = (bf16[4,128,256]{2,1,0:T(8,128)(2,1)S(1)}, bf16[4,128,256]{2,1,0:T(8,128)(2,1)}, u32[]{:S(2)}, u32[]{:S(2)}) collective-permute-start(bf16[4,128,256]{2,1,0:T(8,128)(2,1)S(1)} %bitcast.26), channel_id=1, source_target_pairs={{0,4},{4,8},{8,12},{12,16},{16,20},{20,24},{24,28},{28,32},{32,36}... | collective-permute-start | bytes 786440 | tf_op jit(solution)/shard_map/ppermute | solution.py:15
  38.2 31.2 %collective-permute-start.2 = (bf16[4,128,256]{2,1,0:T(8,128)(2,1)S(1)}, bf16[4,128,256]{2,1,0:T(8,128)(2,1)}, u32[]{:S(2)}, u32[]{:S(2)}) collective-permute-start(bf16[4,128,256]{2,1,0:T(8,128)(2,1)S(1)} %bitcast.27), channel_id=1, source_target_pairs={{0,508},{4,0},{8,4},{12,8},{16,12},{20,16},{24,20},{28,24},{32,28}... | collective-permute-start | bytes 786440 | tf_op jit(solution)/shard_map/ppermute | solution.py:15
  44.2 26.9 %collective-permute-start.3 = (bf16[4,128,256]{2,1,0:T(8,128)(2,1)S(1)}, bf16[4,128,256]{2,1,0:T(8,128)(2,1)}, u32[]{:S(2)}, u32[]{:S(2)}) collective-permute-start(bf16[4,128,256]{2,1,0:T(8,128)(2,1)S(1)} %bitcast.28), channel_id=1, source_target_pairs={{0,504},{4,508},{8,0},{12,4},{16,8},{20,12},{24,16},{28,20},{32,24... | collective-permute-start | bytes 786440 | tf_op jit(solution)/shard_map/ppermute | solution.py:15
  62.0 3.2 %copy-start.1 = (f32[4,4,128,1024]{3,2,1,0:T(8,128)}, f32[4,4,128,1024]{3,2,1,0:T(8,128)S(1)}, u32[]{:S(2)}) copy-start(f32[4,4,128,1024]{3,2,1,0:T(8,128)S(1)} %fusion.4) | copy-start | bytes 25165828
  78.0 12.4 %copy-start.5 = (bf16[256,1024]{1,0:T(8,128)(2,1)S(1)}, bf16[256,1024]{1,0:T(8,128)(2,1)}, u32[]{:S(2)}) copy-start(bf16[256,1024]{1,0:T(8,128)(2,1)} %param.11) | copy-start | bytes 1572868
  90.1 30.9 %copy-start.3 = (bf16[512,1024]{1,0:T(8,128)(2,1)S(1)}, bf16[512,1024]{1,0:T(8,128)(2,1)}, u32[]{:S(2)}) copy-start(bf16[512,1024]{1,0:T(8,128)(2,1)} %param.8) | copy-start | bytes 3145732
  91.8 73.5 %copy-start.7 = (bf16[1024,512]{1,0:T(8,128)(2,1)S(1)}, bf16[1024,512]{1,0:T(8,128)(2,1)}, u32[]{:S(2)}) copy-start(bf16[1024,512]{1,0:T(8,128)(2,1)} %param.13) | copy-start | bytes 3145732
  91.8 73.5 %all-gather.2.cloned.1.call-start = ((), (), s32[]{:S(2)}) async-start(), calls=%async_computation.3 | async-start | bytes 1310720 | tf_op jit(solution)/shard_map/all_gather | solution.py:74
  132.4 69.1 %copy-start.4 = (bf16[512,256]{1,0:T(8,128)(2,1)S(1)}, bf16[512,256]{1,0:T(8,128)(2,1)}, u32[]{:S(2)}) copy-start(bf16[512,256]{1,0:T(8,128)(2,1)} %reduce-scatter.3.cloned.1.call-done) | copy-start | bytes 786436
  132.4 69.1 %reduce-scatter.5.cloned.1.call-start = ((), (), s32[]{:S(2)}) async-start(), calls=%async_computation.4 | async-start | bytes 1310720 | tf_op jit(solution)/shard_map/reduce_scatter | solution.py:79
Sparse Core Ops, SparseCore 0:
  92.0 29.0 reduce-scatter.2
  132.5 32.8 all-gather.1
  169.1 32.3 reduce-scatter.4
where the time goes:
time: 211 us; the launch traced here: 210 us
  waiting for transfers between devices  93.9 us (45%)
  starting transfers between devices  34.6 us (16%)
  local copies, waits for them, and re-layouts  26.8 us (13%)
  matrix products  23.6 us (11%)
  between operations  13.3 us (6%)
  other arithmetic  9.3 us (4%)
  blocking collectives  8.37 us (4%)
    ppermute x8, starting transfers between devices, from_behind(): lax.ppermute(array, axis, [(i, (i + by) % length) for i in range(length)])  34.5 us
    all_gather x1, waiting for transfers between devices, per_device(): normed2 = lax.all_gather(normed_cols, 'mp', axis=1, tiled=True)  32.9 us
    reduce_scatter x1, waiting for transfers between devices, per_device(): lax.psum_scatter(down_term.astype(jnp.bfloat16), 'mp', scatter_dimension=...  32.6 us
    reduce_scatter x1, waiting for transfers between devices, per_device(): lax.psum_scatter(partial_value.astype(jnp.bfloat16), 'mp', scatter_dimens...  28.3 us
    dot_general x1, matrix products, per_device(): jnp.einsum('phqk,pkhd->pqhd', probs, vals_nb, preferred_element_type=jnp....  12.1 us
    unnamed x26, local copies, waits for them, and re-layouts  11.6 us
    psum x1, blocking collectives, per_device(): square_sum = lax.psum(jnp.sum(residual_cols * residual_cols, axis=1), 'mp')  8.37 us
  transfers between devices with their start and end apart: 11, of which 3 were waited for; matrix products, arithmetic and copies ran while one was open for 12% of the time, Pallas kernels for 0%

commit v1 on v0

--- a/solution.py
+++ b/solution.py
@@ -22,6 +22,13 @@
 
 
 def per_device(features, gain_attn, w_qkv, w_out, gain_mlp, w_up, w_down, neighbours):
+
+    def extend_sums_all_here(local_array):
+        mid_arr = lax.all_to_all(
+            jnp.concatenate([local_array] * lax.axis_size("mp"), 1), "mp", 1, 1, tiled=True
+        )
+        return mid_arr
+
     row_count = features.shape[0]
     patches_here = row_count // PN
     heads_here = w_qkv.shape[2] // HD
@@ -71,7 +78,7 @@
     square_sum = lax.psum(jnp.sum(residual_cols * residual_cols, axis=1), "mp")
     inverse_rms = lax.rsqrt(square_sum / D + 1e-05)
     normed_cols = (residual_cols * inverse_rms[:, None] * gain_cols).astype(jnp.bfloat16)
-    normed2 = lax.all_gather(normed_cols, "mp", axis=1, tiled=True)
+    normed2 = extend_sums_all_here(normed_cols)
     hidden = jax.nn.gelu(
         jnp.dot(normed2, w_up, preferred_element_type=jnp.float32), approximate=True
     ).astype(jnp.bfloat16)

time: 211 us -> 192 us (0.910)
  waiting for transfers between devices: 93.9 us -> 59.5 us
  blocking collectives: 8.37 us -> 23 us
    all_gather x1 -> x0, waiting for transfers between devices: 32.9 us -> none  [per_device(): normed2 = lax.all_gather(normed_cols, 'mp', axis=1, tiled=True)]
    all_to_all x0 -> x1, blocking collectives: none -> 14.7 us  [extend_sums_all_here(): lax.all_to_all(jnp.concatenate([local_array] * lax.axis_size('mp'), 1), '...]
    unnamed x26 -> x24, local copies, waits for them, and re-layouts: 11.6 us -> 11.6 us
  transfers between devices with their start and end apart: 11 -> 10, of which waited for: 3 -> 2; matrix products, arithmetic and copies ran while one was open for 12% -> 14% of each run, Pallas kernels for 0% -> 0%
where the time goes in v1:
time: 192 us; the launch traced here: 191 us
  waiting for transfers between devices  59.5 us (31%)
  starting transfers between devices  34.5 us (18%)
  local copies, waits for them, and re-layouts  28.2 us (15%)
  matrix products  24 us (12%)
  blocking collectives  23 us (12%)
  between operations  13.6 us (7%)
  other arithmetic  8.66 us (5%)
    ppermute x8, starting transfers between devices, from_behind(): lax.ppermute(array, axis, [(i, (i + by) % length) for i in range(length)])  34.5 us
    reduce_scatter x1, waiting for transfers between devices, per_device(): lax.psum_scatter(down_term.astype(jnp.bfloat16), 'mp', scatter_dimension=...  31.1 us
    reduce_scatter x1, waiting for transfers between devices, per_device(): lax.psum_scatter(partial_value.astype(jnp.bfloat16), 'mp', scatter_dimens...  28.4 us
    all_to_all x1, blocking collectives, extend_sums_all_here(): lax.all_to_all(jnp.concatenate([local_array] * lax.axis_size('mp'), 1), '...  14.7 us
    dot_general x1, matrix products, per_device(): jnp.einsum('phqk,pkhd->pqhd', probs, vals_nb, preferred_element_type=jnp....  12.1 us
    unnamed x24, local copies, waits for them, and re-layouts  11.6 us
    psum x1, blocking collectives, per_device(): square_sum = lax.psum(jnp.sum(residual_cols * residual_cols, axis=1), 'mp')  8.31 us
    dot_general x1, matrix products, per_device(): down_term = jnp.dot(hidden, w_down, preferred_element_type=jnp.float32)  3.97 us
  transfers between devices with their start and end apart: 10, of which 2 were waited for; matrix products, arithmetic and copies ran while one was open for 14% of the time, Pallas kernels for 0%

profile of v1, /device:TPU:8, one launch (start us, length us, event | category | flops | bytes accessed | tf_op | source)
XLA Modules:
  0.0 191.4 jit_solution(1558125088424479848)
XLA Ops:
  6.5 0.0 copy-start.6
  6.6 1.7 fusion.9
  8.2 1.9 convolution_convert_fusion.2
  10.1 3.5 %collective-permute-start.4 = (bf16[4,128,256]{2,1,0:T(8,128)(2,1)S(1)}, bf16[4,128,256]{2,1,0:T(8,128)(2,1)}, u32[]{:S(2)}, u32[]{:S(2)}) collective-permute-start(bf16[4,128,256]{2,1,0:T(8,128)(2,1)S(1)} %bitcast.38), channel_id=1, source_target_pairs={{0,8},{4,12},{8,16},{12,20},{16,24},{20,28},{24,32},{28,36},{32,40... | collective-permute-start | bytes 786440 | tf_op jit(solution)/shard_map/ppermute | solution.py:15
  13.6 1.9 %collective-permute-start.5 = (bf16[4,128,256]{2,1,0:T(8,128)(2,1)S(1)}, bf16[4,128,256]{2,1,0:T(8,128)(2,1)}, u32[]{:S(2)}, u32[]{:S(2)}) collective-permute-start(bf16[4,128,256]{2,1,0:T(8,128)(2,1)S(1)} %bitcast.39), channel_id=1, source_target_pairs={{0,4},{4,8},{8,12},{12,16},{16,20},{20,24},{24,28},{28,32},{32,36}... | collective-permute-start | bytes 786440 | tf_op jit(solution)/shard_map/ppermute | solution.py:15
  15.5 3.6 %collective-permute-start.6 = (bf16[4,128,256]{2,1,0:T(8,128)(2,1)S(1)}, bf16[4,128,256]{2,1,0:T(8,128)(2,1)S(1)}, u32[]{:S(2)}, u32[]{:S(2)}) collective-permute-start(bf16[4,128,256]{2,1,0:T(8,128)(2,1)S(1)} %bitcast.40), channel_id=1, source_target_pairs={{0,508},{4,0},{8,4},{12,8},{16,12},{20,16},{24,20},{28,24},{32,28}... | collective-permute-start | bytes 786440 | tf_op jit(solution)/shard_map/ppermute | solution.py:15
  19.2 10.4 %collective-permute-start.7 = (bf16[4,128,256]{2,1,0:T(8,128)(2,1)S(1)}, bf16[4,128,256]{2,1,0:T(8,128)(2,1)S(1)}, u32[]{:S(2)}, u32[]{:S(2)}) collective-permute-start(bf16[4,128,256]{2,1,0:T(8,128)(2,1)S(1)} %bitcast.41), channel_id=1, source_target_pairs={{0,504},{4,508},{8,0},{12,4},{16,8},{20,12},{24,16},{28,20},{32,24... | collective-permute-start | bytes 786440 | tf_op jit(solution)/shard_map/ppermute | solution.py:15
  29.6 0.0 copy-done.2
  29.6 0.0 copy-done.7
  29.6 0.0 copy-done.6
  29.7 0.5 convolution_convert_fusion.4
  30.1 1.9 %collective-permute-start = (bf16[4,128,256]{2,1,0:T(8,128)(2,1)S(1)}, bf16[4,128,256]{2,1,0:T(8,128)(2,1)}, u32[]{:S(2)}, u32[]{:S(2)}) collective-permute-start(bf16[4,128,256]{2,1,0:T(8,128)(2,1)S(1)} %bitcast.33), channel_id=1, source_target_pairs={{0,8},{4,12},{8,16},{12,20},{16,24},{20,28},{24,32},{28,36},{32,40... | collective-permute-start | bytes 786440 | tf_op jit(solution)/shard_map/ppermute | solution.py:15
  32.1 0.5 convolution_convert_fusion.3
  32.6 0.8 compare_select_fusion
  33.4 0.1 copy.34
  33.5 0.1 reshape.41
  33.5 1.0 reshape.62
  34.6 0.0 collective-permute-done.4
  34.6 1.9 %collective-permute-start.1 = (bf16[4,128,256]{2,1,0:T(8,128)(2,1)S(1)}, bf16[4,128,256]{2,1,0:T(8,128)(2,1)}, u32[]{:S(2)}, u32[]{:S(2)}) collective-permute-start(bf16[4,128,256]{2,1,0:T(8,128)(2,1)S(1)} %bitcast.34), channel_id=1, source_target_pairs={{0,4},{4,8},{8,12},{12,16},{16,20},{20,24},{24,28},{28,32},{32,36}... | collective-permute-start | bytes 786440 | tf_op jit(solution)/shard_map/ppermute | solution.py:15
  36.5 1.7 constant_dynamic-update-slice_fusion.9
  38.2 0.0 collective-permute-done.5
  38.2 3.6 %collective-permute-start.2 = (bf16[4,128,256]{2,1,0:T(8,128)(2,1)S(1)}, bf16[4,128,256]{2,1,0:T(8,128)(2,1)}, u32[]{:S(2)}, u32[]{:S(2)}) collective-permute-start(bf16[4,128,256]{2,1,0:T(8,128)(2,1)S(1)} %bitcast.35), channel_id=1, source_target_pairs={{0,508},{4,0},{8,4},{12,8},{16,12},{20,16},{24,20},{28,24},{32,28}... | collective-permute-start | bytes 786440 | tf_op jit(solution)/shard_map/ppermute | solution.py:15
  41.8 1.7 constant_dynamic-update-slice_fusion.8
  43.5 0.7 constant_dynamic-update-slice_fusion.7
  44.2 0.0 collective-permute-done.6
  44.2 7.5 %collective-permute-start.3 = (bf16[4,128,256]{2,1,0:T(8,128)(2,1)S(1)}, bf16[4,128,256]{2,1,0:T(8,128)(2,1)}, u32[]{:S(2)}, u32[]{:S(2)}) collective-permute-start(bf16[4,128,256]{2,1,0:T(8,128)(2,1)S(1)} %bitcast.36), channel_id=1, source_target_pairs={{0,504},{4,508},{8,0},{12,4},{16,8},{20,12},{24,16},{28,20},{32,24... | collective-permute-start | bytes 786440 | tf_op jit(solution)/shard_map/ppermute | solution.py:15
  51.7 0.7 constant_dynamic-update-slice_fusion.6
  52.5 0.0 collective-permute-done.7
  52.5 0.7 constant_dynamic-update-slice_fusion.5
  53.2 2.0 %gather_fusion.1 = bf16[32,128,256]{2,1,0:T(8,128)(2,1)S(1)} fusion(bf16[20,128,256]{2,1,0:T(8,128)(2,1)} %constant_dynamic-update-slice_fusion.5, s32[1024]{0:T(1024)S(1)} %pad_clamp_fusion), kind=kCustom, calls=%fused_computation.1 | custom fusion | bytes 4194432 | tf_op jit(solution)/shard_map/gather | solution.py:59
  55.2 3.3 %reshape.63 = bf16[4,1024,4,64]{3,2,1,0:T(4,128)(2,1)} reshape(bf16[32,128,256]{2,1,0:T(8,128)(2,1)S(1)} %gather_fusion.1) | data formatting | bytes 4194304 | tf_op jit(solution)/shard_map/reshape | solution.py:59
  58.5 3.6 %fusion.4 = f32[4,4,128,1024]{3,2,1,0:T(8,128)S(1)} fusion(bf16[4,1024,4,64]{3,2,1,0:T(4,128)(2,1)} %reshape.63, bf16[4,128,4,64]{3,2,1,0:T(4,128)(2,1)} %reshape.62), kind=kOutput, calls=%fused_computation.7 | convolution fusion | flops 268435456 | bytes 10747904 | tf_op jit(solution)/shard_map/pqhd,pkhd->phqk/dot_general | solution.py:62
  62.1 2.2 %fusion.62 = f32[4,4,128]{2,1,0:T(4,128)S(1)} fusion(f32[4,4,128,1024]{3,2,1,0:T(8,128)S(1)} %fusion.4), kind=kOutput, calls=%fused_computation.89 | output fusion | flops 8389631 | bytes 8396800 | tf_op jit(solution)/shard_map/sub | solution.py:65
  64.3 1.0 copy-done.1
  65.3 0.0 collective-permute-done
  65.3 1.7 constant_dynamic-update-slice_fusion.4
  67.0 0.0 collective-permute-done.1
  67.0 1.7 constant_dynamic-update-slice_fusion.3
  68.7 0.7 constant_dynamic-update-slice_fusion.2
  69.4 0.0 collective-permute-done.2
  69.4 1.7 constant_dynamic-update-slice_fusion.1
  71.1 0.0 collective-permute-done.3
  71.1 1.7 constant_dynamic-update-slice_fusion
  72.8 2.0 %gather_fusion = bf16[32,128,256]{2,1,0:T(8,128)(2,1)S(1)} fusion(bf16[20,128,256]{2,1,0:T(8,128)(2,1)} %constant_dynamic-update-slice_fusion, s32[1024]{0:T(1024)S(1)} %pad_clamp_fusion), kind=kCustom, calls=%fused_computation | custom fusion | bytes 4194432 | tf_op jit(solution)/shard_map/gather | solution.py:60
  74.8 3.3 %reshape.61 = bf16[4,1024,4,64]{3,2,1,0:T(4,128)(2,1)} reshape(bf16[32,128,256]{2,1,0:T(8,128)(2,1)S(1)} %gather_fusion) | data formatting | bytes 4194304 | tf_op jit(solution)/shard_map/reshape | solution.py:60
  78.1 12.1 %fusion.15 = bf16[4,128,4,64]{1,3,2,0:T(8,128)(2,1)S(1)} fusion(f32[4,4,128]{2,1,0:T(4,128)S(1)} %fusion.62, bf16[4,1024,4,64]{3,2,1,0:T(4,128)(2,1)} %reshape.61, f32[4,4,128,1024]{3,2,1,0:T(8,128)} %copy-done.1), kind=kOutput, calls=%fused_computation.24 | convolution fusion | flops 279055360 | bytes 10756096 | tf_op jit(solution)/shard_map/phqk,pkhd->pqhd/dot_general | solution.py:66
  90.2 0.0 copy-start.3
  90.2 0.2 copy.41
  90.4 1.5 convolution_convert_fusion
  91.9 0.0 reduce-scatter.3.cloned.1.call-update
  91.9 0.0 reduce-scatter.5.cloned.1.call-start
  92.0 0.8 dynamic_slice.11
  92.7 28.4 %reduce-scatter.3.cloned.1.call-done = bf16[512,256]{1,0:T(8,128)(2,1)} async-done(((bf16[512,1024]{1,0:T(8,128)(2,1)}), bf16[512,256]{1,0:T(8,128)(2,1)}) %reduce-scatter.3.cloned.1.call-update) | async-done | bytes 262160 | tf_op jit(solution)/shard_map/reduce_scatter | solution.py:69
  121.1 1.1 multiply_reduce_fusion.1
  122.2 8.3 %psum.7 = f32[512]{0:T(512)S(1)} all-reduce(f32[512]{0:T(512)S(1)} %multiply_reduce_fusion.1), channel_id=1, replica_groups=mesh['patch'=128,'mp'=4] {'mp'}, use_global_device_ids=true, to_apply=%region_5.6 | all-reduce | flops 512 | bytes 4096 | tf_op jit(solution)/shard_map/psum | solution.py:78
  130.5 1.1 multiply_convert_fusion
  131.6 0.1 pad_maximum_fusion
  131.7 0.1 copy.67
  131.8 14.7 %all_to_all.12 = bf16[512,4,256]{2,0,1:T(8,128)(2,1)S(1)} all-to-all(bf16[512,4,256]{2,0,1:T(8,128)(2,1)S(1)} %bitcast.30), channel_id=1, replica_groups=mesh['patch'=128,'mp'=4] {'mp'}, dimensions={1} | all-to-all | bytes 2097152 | tf_op jit(solution)/shard_map/all_to_all | solution.py:27
  146.5 1.3 copy.43
  147.8 4.0 %convolution_convert_fusion.1 = bf16[512,1024]{1,0:T(8,128)(2,1)} fusion(bf16[512,1024]{1,0:T(8,128)(2,1)S(1)} %copy-done, bf16[512,1024]{0,1:T(8,128)(2,1)} %bitcast.32, bf16[1024,512]{1,0:T(8,128)(2,1)} %param.13), kind=kOutput, calls=%fused_computation.19 | convolution fusion | flops 1076625408 | bytes 4194304 | tf_op jit(solution)/shard_map/dot_general | solution.py:85
  151.8 0.0 reduce-scatter.5.cloned.1.call-update
  151.8 31.1 %reduce-scatter.5.cloned.1.call-done = bf16[512,256]{1,0:T(8,128)(2,1)} async-done(((bf16[512,1024]{1,0:T(8,128)(2,1)}), bf16[512,256]{1,0:T(8,128)(2,1)}) %reduce-scatter.5.cloned.1.call-update) | async-done | bytes 262160 | tf_op jit(solution)/shard_map/reduce_scatter | solution.py:86
  182.9 1.8 add_convert_fusion
  (14 shorter events, 0.0 us)
Async XLA Ops:
  6.5 141.3 %copy-start = (bf16[512,1024]{1,0:T(8,128)(2,1)S(1)}, bf16[512,1024]{1,0:T(8,128)(2,1)}, u32[]{:S(2)}) copy-start(bf16[512,1024]{1,0:T(8,128)(2,1)} %param.14) | copy-start | bytes 3145732
  6.5 23.1 %copy-start.2 = (bf16[512,1024]{1,0:T(8,128)(2,1)S(1)}, bf16[512,1024]{1,0:T(8,128)(2,1)}, u32[]{:S(2)}) copy-start(bf16[512,1024]{1,0:T(8,128)(2,1)} %param.8) | copy-start | bytes 3145732
  6.5 23.1 %copy-start.7 = (f32[1024]{0:T(1024)S(1)}, f32[1024]{0:T(1024)}, u32[]{:S(2)}) copy-start(f32[1024]{0:T(1024)} %param.9) | copy-start | bytes 12292
  6.5 114.6 %reduce-scatter.3.cloned.1.call-start = ((), (), s32[]{:S(2)}) async-start(), calls=%async_computation.3 | async-start | bytes 1310720 | tf_op jit(solution)/shard_map/reduce_scatter | solution.py:69
  6.5 23.1 %copy-start.6 = (bf16[3,1024,256]{2,1,0:T(8,128)(2,1)S(1)}, bf16[3,1024,256]{2,1,0:T(8,128)(2,1)}, u32[]{:S(2)}) copy-start(bf16[3,1024,256]{2,1,0:T(8,128)(2,1)} %param.10) | copy-start | bytes 4718596
  10.1 24.5 %collective-permute-start.4 = (bf16[4,128,256]{2,1,0:T(8,128)(2,1)S(1)}, bf16[4,128,256]{2,1,0:T(8,128)(2,1)}, u32[]{:S(2)}, u32[]{:S(2)}) collective-permute-start(bf16[4,128,256]{2,1,0:T(8,128)(2,1)S(1)} %bitcast.38), channel_id=1, source_target_pairs={{0,8},{4,12},{8,16},{12,20},{16,24},{20,28},{24,32},{28,36},{32,40... | collective-permute-start | bytes 786440 | tf_op jit(solution)/shard_map/ppermute | solution.py:15
  13.6 24.6 %collective-permute-start.5 = (bf16[4,128,256]{2,1,0:T(8,128)(2,1)S(1)}, bf16[4,128,256]{2,1,0:T(8,128)(2,1)}, u32[]{:S(2)}, u32[]{:S(2)}) collective-permute-start(bf16[4,128,256]{2,1,0:T(8,128)(2,1)S(1)} %bitcast.39), channel_id=1, source_target_pairs={{0,4},{4,8},{8,12},{12,16},{16,20},{20,24},{24,28},{28,32},{32,36}... | collective-permute-start | bytes 786440 | tf_op jit(solution)/shard_map/ppermute | solution.py:15
  15.5 28.7 %collective-permute-start.6 = (bf16[4,128,256]{2,1,0:T(8,128)(2,1)S(1)}, bf16[4,128,256]{2,1,0:T(8,128)(2,1)S(1)}, u32[]{:S(2)}, u32[]{:S(2)}) collective-permute-start(bf16[4,128,256]{2,1,0:T(8,128)(2,1)S(1)} %bitcast.40), channel_id=1, source_target_pairs={{0,508},{4,0},{8,4},{12,8},{16,12},{20,16},{24,20},{28,24},{32,28}... | collective-permute-start | bytes 786440 | tf_op jit(solution)/shard_map/ppermute | solution.py:15
  19.2 33.3 %collective-permute-start.7 = (bf16[4,128,256]{2,1,0:T(8,128)(2,1)S(1)}, bf16[4,128,256]{2,1,0:T(8,128)(2,1)S(1)}, u32[]{:S(2)}, u32[]{:S(2)}) collective-permute-start(bf16[4,128,256]{2,1,0:T(8,128)(2,1)S(1)} %bitcast.41), channel_id=1, source_target_pairs={{0,504},{4,508},{8,0},{12,4},{16,8},{20,12},{24,16},{28,20},{32,24... | collective-permute-start | bytes 786440 | tf_op jit(solution)/shard_map/ppermute | solution.py:15
  30.1 35.2 %collective-permute-start = (bf16[4,128,256]{2,1,0:T(8,128)(2,1)S(1)}, bf16[4,128,256]{2,1,0:T(8,128)(2,1)}, u32[]{:S(2)}, u32[]{:S(2)}) collective-permute-start(bf16[4,128,256]{2,1,0:T(8,128)(2,1)S(1)} %bitcast.33), channel_id=1, source_target_pairs={{0,8},{4,12},{8,16},{12,20},{16,24},{20,28},{24,32},{28,36},{32,40... | collective-permute-start | bytes 786440 | tf_op jit(solution)/shard_map/ppermute | solution.py:15
  34.6 32.4 %collective-permute-start.1 = (bf16[4,128,256]{2,1,0:T(8,128)(2,1)S(1)}, bf16[4,128,256]{2,1,0:T(8,128)(2,1)}, u32[]{:S(2)}, u32[]{:S(2)}) collective-permute-start(bf16[4,128,256]{2,1,0:T(8,128)(2,1)S(1)} %bitcast.34), channel_id=1, source_target_pairs={{0,4},{4,8},{8,12},{12,16},{16,20},{20,24},{24,28},{28,32},{32,36}... | collective-permute-start | bytes 786440 | tf_op jit(solution)/shard_map/ppermute | solution.py:15
  38.2 31.2 %collective-permute-start.2 = (bf16[4,128,256]{2,1,0:T(8,128)(2,1)S(1)}, bf16[4,128,256]{2,1,0:T(8,128)(2,1)}, u32[]{:S(2)}, u32[]{:S(2)}) collective-permute-start(bf16[4,128,256]{2,1,0:T(8,128)(2,1)S(1)} %bitcast.35), channel_id=1, source_target_pairs={{0,508},{4,0},{8,4},{12,8},{16,12},{20,16},{24,20},{28,24},{32,28}... | collective-permute-start | bytes 786440 | tf_op jit(solution)/shard_map/ppermute | solution.py:15
  44.2 26.9 %collective-permute-start.3 = (bf16[4,128,256]{2,1,0:T(8,128)(2,1)S(1)}, bf16[4,128,256]{2,1,0:T(8,128)(2,1)}, u32[]{:S(2)}, u32[]{:S(2)}) collective-permute-start(bf16[4,128,256]{2,1,0:T(8,128)(2,1)S(1)} %bitcast.36), channel_id=1, source_target_pairs={{0,504},{4,508},{8,0},{12,4},{16,8},{20,12},{24,16},{28,20},{32,24... | collective-permute-start | bytes 786440 | tf_op jit(solution)/shard_map/ppermute | solution.py:15
  62.1 3.2 %copy-start.1 = (f32[4,4,128,1024]{3,2,1,0:T(8,128)}, f32[4,4,128,1024]{3,2,1,0:T(8,128)S(1)}, u32[]{:S(2)}) copy-start(f32[4,4,128,1024]{3,2,1,0:T(8,128)S(1)} %fusion.4) | copy-start | bytes 25165828
  78.1 12.4 %copy-start.5 = (bf16[256,1024]{1,0:T(8,128)(2,1)S(1)}, bf16[256,1024]{1,0:T(8,128)(2,1)}, u32[]{:S(2)}) copy-start(bf16[256,1024]{1,0:T(8,128)(2,1)} %param.11) | copy-start | bytes 1572868
  90.2 30.9 %copy-start.3 = (bf16[512,1024]{1,0:T(8,128)(2,1)S(1)}, bf16[512,1024]{1,0:T(8,128)(2,1)}, u32[]{:S(2)}) copy-start(bf16[512,1024]{1,0:T(8,128)(2,1)} %param.8) | copy-start | bytes 3145732
  91.9 90.9 %reduce-scatter.5.cloned.1.call-start = ((), (), s32[]{:S(2)}) async-start(), calls=%async_computation.4 | async-start | bytes 1310720 | tf_op jit(solution)/shard_map/reduce_scatter | solution.py:86
  147.8 35.1 %copy-start.4 = (bf16[512,256]{1,0:T(8,128)(2,1)S(1)}, bf16[512,256]{1,0:T(8,128)(2,1)}, u32[]{:S(2)}) copy-start(bf16[512,256]{1,0:T(8,128)(2,1)} %reduce-scatter.3.cloned.1.call-done) | copy-start | bytes 786436
Sparse Core Ops, SparseCore 0:
  92.0 29.0 reduce-scatter.2
  151.9 30.8 reduce-scatter.4
